TPU v7x, 32 devices: a whole 2x2x4 slice. The times are simulated.
32 devices in a mesh: dp: 8 (over z, x), group: 4 (over y, core).
Axes of the slice: x: 2, y: 2, z: 4, core: 2. Of those that a mesh axis runs over, the one named last changes fastest.
Arguments:
- partials: float32 [4, 54, 1024, 1024], P('group', None, 'dp'), may hold values from -0.3 to 0.3
- second_moment: float32 [54, 1024, 1024], P(None, 'dp', 'group'), may hold values from 0.0001 to 0.01
- left_stats: float32 [54, 1024, 1024], P(None, 'dp', 'group'), may hold values from -3 to 3
- right_stats: float32 [54, 1024, 1024], P(None, 'dp', 'group'), may hold values from -3 to 3
- left_roots: bfloat16 [54, 1024, 1024], P(None, 'dp', 'group'), may hold values from -0.2 to 2.1
- right_roots: bfloat16 [54, 1024, 1024], P(None, 'dp', 'group'), may hold values from -0.2 to 2.1
- norm_partials: float32 [8, 4, 2, 2048], P('dp', 'group'), may hold values from -0.012 to 0.012
- norm_moment: float32 [2, 2048], replicated, may hold values from 0.0001 to 0.01
Outputs:
- block_step: bfloat16 [54, 1024, 1024], P(None, 'dp', 'group')
- new_moment: float32 [54, 1024, 1024], P(None, 'dp', 'group')
- new_left: float32 [54, 1024, 1024], P(None, 'dp', 'group')
- new_right: float32 [54, 1024, 1024], P(None, 'dp', 'group')
- norm_step: float32 [2, 2048], replicated
- new_norm_moment: float32 [2, 2048], replicated
All inputs are finite; a program needn't handle non-finite values.
Results may differ from a plain program's by a relative error of at most 0.0042.
The roundings to bfloat16 on the way count: a program that leaves them out, or rounds other values in their place, can miss the bound.
Values may be sent and summed in bfloat16 or wider, within the bound.
No kernel may reach another device: no remote copies, remote signals or barrier semaphores. Data moves between devices by JAX's collectives and lax.ppermute only.
A program may use at most 384 MiB of HBM per device.

v0:
```python
import jax
import jax.numpy as jnp
from jax import lax
from jax.sharding import PartitionSpec as P

EPS_ADAM = 1e-08
EPS_GRAFT = 1e-06


def on_device(
    partials,
    second_moment,
    left_stats,
    right_stats,
    left_roots,
    right_roots,
    norm_partials,
    norm_moment,
):
    n_dp = lax.axis_size("dp")
    me_dp = lax.axis_index("dp")
    me_group = lax.axis_index("group")
    count = second_moment.shape[0]
    rows = partials.shape[2]
    quarter = second_moment.shape[2]
    width = rows * n_dp
    cap = -(-count // n_dp)
    slots = cap * n_dp
    lower = me_group * quarter

    def to_owners(blocks):
        padded = jnp.pad(blocks, ((0, slots - count), (0, 0), (0, 0)))
        sent = lax.all_to_all(padded.reshape(n_dp, cap, rows, quarter), "dp", 0, 0, tiled=True)
        return sent.transpose(1, 0, 2, 3).reshape(cap, width, quarter)

    def to_keepers(owned):
        back = lax.all_to_all(owned, "dp", 0, 0, tiled=True)
        return back.reshape(slots, rows, quarter)[:count]

    left_root = to_owners(left_roots)
    right_root = to_owners(right_roots)
    local_norm = norm_partials[0, 0]
    norm_grad = jnp.sum(lax.all_gather(local_norm, ("dp", "group")), axis=0)
    grad = lax.psum_scatter(partials[0], "group", scatter_dimension=2, tiled=True)
    grad, left_root, right_root = lax.optimization_barrier((grad, left_root, right_root))
    new_moment = 0.99 * second_moment + 0.01 * grad * grad
    adam = grad / (jnp.sqrt(new_moment) + EPS_ADAM)
    adam_part = jnp.sum(adam * adam, axis=(1, 2))
    adam_sq = jnp.sum(lax.all_gather(adam_part, ("dp", "group")), axis=0)
    grad_low = grad.astype(jnp.bfloat16)
    mine = to_owners(grad_low)
    piece = lax.all_gather(mine, "group", axis=2, tiled=True)
    own_rows = lax.dynamic_slice_in_dim(piece, lower, quarter, 1)
    piece4 = piece.reshape(cap, n_dp, rows, width)
    gram_left = jnp.einsum("cdim,cjm->dcij", piece4, own_rows, preferred_element_type=jnp.float32)
    gram_right = jnp.einsum("cim,cij->cmj", piece, mine, preferred_element_type=jnp.float32)
    gram_right = gram_right.reshape(cap, n_dp, rows, quarter).transpose(1, 0, 2, 3)
    left_term = to_keepers(gram_left.astype(jnp.bfloat16)).astype(jnp.float32)
    right_term = to_keepers(gram_right.astype(jnp.bfloat16)).astype(jnp.float32)
    half = jnp.einsum("cim,cmj->cij", piece, right_root, preferred_element_type=jnp.float32)
    half = half.astype(jnp.bfloat16)
    full_left = lax.all_gather(left_root, "group", axis=2, tiled=True)
    full_left4 = full_left.reshape(cap, n_dp, rows, width)
    direction = jnp.einsum("cdim,cmj->dcij", full_left4, half, preferred_element_type=jnp.float32)
    direction_sq = lax.psum(jnp.sum(direction * direction, axis=(0, 2, 3)), "group")
    adam_pad = jnp.pad(adam_sq, (0, slots - count))
    adam_owned = lax.dynamic_slice_in_dim(adam_pad, me_dp * cap, cap)
    ratio = jnp.sqrt(adam_owned / (direction_sq + EPS_GRAFT))
    scaled = (ratio[None, :, None, None] * direction).astype(jnp.bfloat16)
    block_step = to_keepers(scaled)
    new_left = 0.95 * left_stats + 0.05 * left_term
    new_right = 0.95 * right_stats + 0.05 * right_term
    new_norm_moment = 0.99 * norm_moment + 0.01 * norm_grad * norm_grad
    norm_step = norm_grad / (jnp.sqrt(new_norm_moment) + EPS_ADAM)
    return (block_step, new_moment, new_left, new_right, norm_step, new_norm_moment)


def solution(mesh):
    return jax.shard_map(
        on_device,
        mesh=mesh,
        in_specs=(
            P("group", None, "dp", None),
            P(None, "dp", "group"),
            P(None, "dp", "group"),
            P(None, "dp", "group"),
            P(None, "dp", "group"),
            P(None, "dp", "group"),
            P("dp", "group", None, None),
            P(),
        ),
        out_specs=(
            P(None, "dp", "group"),
            P(None, "dp", "group"),
            P(None, "dp", "group"),
            P(None, "dp", "group"),
            P(),
            P(),
        ),
        check_vma=False,
    )
```

profile of v0, /device:TPU:17, one launch (start us, length us, event | category | flops | bytes accessed | tf_op | source)
XLA Modules:
  0.0 766.6 jit_solution(13714949214837697143)
XLA Ops:
  7.2 0.0 reduce-scatter.2.cloned.1.call-start
  7.2 0.7 reduce-scatter.2.cloned.1.call-update
  7.9 1.3 copy-done
  9.2 2.2 pad.14
  11.4 5.8 all-to-all-start
  17.3 2.2 pad.15
  19.5 75.9 %all-to-all-done = bf16[8,7,128,256]{3,2,1,0:T(8,128)(2,1)} async-done(((bf16[8,7,128,256]{3,2,1,0:T(8,128)(2,1)}), bf16[8,7,128,256]{3,2,1,0:T(8,128)(2,1)}, u32[]{:S(2)}, u32[]{:S(2)}) %all-to-all-start) | async-done | bytes 3670048 | tf_op jit(solution)/shard_map/all_to_all | solution.py:33
  95.4 7.8 %all-to-all-start.1 = ((bf16[8,7,128,256]{3,2,1,0:T(8,128)(2,1)}), bf16[8,7,128,256]{3,2,1,0:T(8,128)(2,1)}, u32[]{:S(2)}, u32[]{:S(2)}) async-start(bf16[8,7,128,256]{3,2,1,0:T(8,128)(2,1)} %bitcast.44), calls=%async_computation.2 | async-start | bytes 7340032 | tf_op jit(solution)/shard_map/all_to_all | solution.py:33
  103.1 4.3 copy.42
  107.4 73.2 %all-to-all-done.1 = bf16[8,7,128,256]{3,2,1,0:T(8,128)(2,1)} async-done(((bf16[8,7,128,256]{3,2,1,0:T(8,128)(2,1)}), bf16[8,7,128,256]{3,2,1,0:T(8,128)(2,1)}, u32[]{:S(2)}, u32[]{:S(2)}) %all-to-all-start.1) | async-done | bytes 3670048 | tf_op jit(solution)/shard_map/all_to_all | solution.py:33
  180.7 4.3 copy.43
  184.9 27.7 %reduce-scatter.2.cloned.1.call-done = f32[54,128,256]{2,1,0:T(8,128)} async-done(((f32[54,128,1024]{2,1,0:T(8,128)}), f32[54,128,256]{2,1,0:T(8,128)}) %reduce-scatter.2.cloned.1.call-update) | async-done | bytes 7077904 | tf_op jit(solution)/shard_map/reduce_scatter | solution.py:44
  212.6 0.0 all-gather.7.cloned.1.call-update
  212.7 0.0 all-gather.5.cloned.1.call-start
  212.7 11.8 %multiply_reduce_fusion.1 = (f32[54]{0:T(128)S(1)}, f32[54,128,256]{2,1,0:T(8,128)}, bf16[54,128,256]{2,1,0:T(8,128)(2,1)S(1)}) fusion(f32[54,128,256]{2,1,0:T(8,128)} %reduce-scatter.2.cloned.1.call-done, f32[54,128,256]{2,1,0:T(8,128)} %param.9), kind=kLoop, calls=%fused_computation.6 | loop fusion | flops 15925194 | bytes 24772824 | tf_op jit(solution)/shard_map/reduce_sum | solution.py:48
  224.5 0.5 pad.17
  225.0 85.1 %all_to_all.30 = bf16[8,7,128,256]{3,2,1,0:T(8,128)(2,1)S(1)} all-to-all(bf16[8,7,128,256]{3,2,1,0:T(8,128)(2,1)S(1)} %bitcast.46), channel_id=1, replica_groups=mesh['dp'=8,'group'=4] {'dp'}, dimensions={0} | all-to-all | bytes 7340032 | tf_op jit(solution)/shard_map/all_to_all | solution.py:33
  310.1 2.3 copy.44
  312.4 0.0 all-gather.5.cloned.1.call-update
  312.4 0.3 dynamic-update-slice
  312.7 40.1 %all-reduce.4 = f32[1728]{0:T(1024)S(1)} all-reduce(f32[1728]{0:T(1024)S(1)} %dynamic-update-slice), channel_id=2, replica_groups=mesh['dp'=8,'group'=4] {'dp','group'}, use_global_device_ids=true, to_apply=%add.4 | all-reduce | flops 1728 | bytes 13824
  352.8 0.1 reshape.59
  352.9 0.0 all-gather.7.cloned.1.call-done
  353.0 57.4 %all-gather.5.cloned.1.call-done = bf16[7,1024,1024]{2,1,0:T(8,128)(2,1)} async-done(((bf16[7,1024,256]{2,1,0:T(8,128)(2,1)}), bf16[7,1024,1024]{2,1,0:T(8,128)(2,1)}) %all-gather.5.cloned.1.call-update) | async-done | bytes 14680080 | tf_op jit(solution)/shard_map/all_gather | solution.py:52
  410.4 17.6 %multiply_reduce_fusion = (f32[7]{0:T(128)S(1)}, f32[7,256,8,128]{3,1,2,0:T(8,128)}) fusion(bf16[7,8,128,1024]{3,2,1,0:T(8,128)(2,1)} %bitcast.57, bf16[7,1024,1024]{2,1,0:T(8,128)(2,1)} %all-gather.5.cloned.1.call-done, bf16[7,1024,256]{2,1,0:T(8,128)(2,1)} %bitcast.54), kind=kOutput, calls=%fused_computation.2 | convolution fusion | flops 7521697792 | bytes 40370204 | tf_op jit(solution)/shard_map/cdim,cmj->dcij/dot_general | solution.py:64
  427.9 5.2 psum.7
  433.2 0.1 fusion.13
  433.3 4.1 fusion.1
  437.4 2.3 copy.46
  439.6 5.4 all-to-all-start.3
  445.0 8.5 %convert_bitcast_fusion = bf16[8,7,128,256]{2,3,0,1:T(8,128)(2,1)S(1)} fusion(bf16[7,8,128,1024]{3,2,1,0:T(8,128)(2,1)} %bitcast.56, bf16[7,1024,1024]{2,1,0:T(8,128)(2,1)} %all-gather.5.cloned.1.call-done, s32[]{:T(128)S(6)} %select_n.7), kind=kOutput, calls=%fused_computation.13 | convolution fusion | flops 3759931392 | bytes 22020100 | tf_op jit(solution)/shard_map/cdim,cjm->dcij/dot_general | solution.py:55
  453.5 2.1 copy.48
  455.6 67.1 %all-to-all-done.3 = bf16[8,7,128,256]{2,3,1,0:T(8,128)(2,1)} async-done(((bf16[8,7,128,256]{2,3,1,0:T(8,128)(2,1)}), bf16[8,7,128,256]{2,3,1,0:T(8,128)(2,1)}, u32[]{:S(2)}, u32[]{:S(2)}) %all-to-all-start.3) | async-done | bytes 3670048 | tf_op jit(solution)/shard_map/all_to_all | solution.py:37
  522.8 8.1 %all-to-all-start.4 = ((bf16[8,7,128,256]{2,3,1,0:T(8,128)(2,1)}), bf16[8,7,128,256]{2,3,1,0:T(8,128)(2,1)}, u32[]{:S(2)}, u32[]{:S(2)}) async-start(bf16[8,7,128,256]{2,3,1,0:T(8,128)(2,1)} %copy.48), calls=%async_computation.5 | async-start | bytes 7340032 | tf_op jit(solution)/shard_map/all_to_all | solution.py:37
  530.9 9.0 %convolution_convert_fusion = bf16[7,1024,256]{2,1,0:T(8,128)(2,1)S(1)} fusion(bf16[7,1024,1024]{2,1,0:T(8,128)(2,1)} %all-gather.5.cloned.1.call-done, bf16[7,1024,256]{2,1,0:T(8,128)(2,1)} %bitcast.48), kind=kOutput, calls=%fused_computation.17 | convolution fusion | flops 3759931392 | bytes 22020096 | tf_op jit(solution)/shard_map/cim,cij->cmj/dot_general | solution.py:56
  539.9 0.0 copy-start.2
  539.9 0.0 copy-start.3
  539.9 2.0 copy.58
  542.0 66.3 %all-to-all-done.4 = bf16[8,7,128,256]{2,3,1,0:T(8,128)(2,1)} async-done(((bf16[8,7,128,256]{2,3,1,0:T(8,128)(2,1)}), bf16[8,7,128,256]{2,3,1,0:T(8,128)(2,1)}, u32[]{:S(2)}, u32[]{:S(2)}) %all-to-all-start.4) | async-done | bytes 3670048 | tf_op jit(solution)/shard_map/all_to_all | solution.py:37
  608.2 8.5 %all-to-all-start.5 = ((bf16[8,7,128,256]{3,2,1,0:T(8,128)(2,1)}), bf16[8,7,128,256]{3,2,1,0:T(8,128)(2,1)}, u32[]{:S(2)}, u32[]{:S(2)}) async-start(bf16[8,7,128,256]{3,2,1,0:T(8,128)(2,1)} %bitcast.50), calls=%async_computation.6 | async-start | bytes 7340032 | tf_op jit(solution)/shard_map/all_to_all | solution.py:37
  616.8 108.7 %all-gather.1 = f32[32,1,2,2048]{3,2,1,0:T(2,128)S(1)} all-gather(f32[1,1,2,2048]{3,2,1,0:T(2,128)S(1)} %copy-done.2), channel_id=3, replica_groups=mesh['dp'=8,'group'=4] {'dp','group'}, dimensions={0}, use_global_device_ids=true | all-gather | bytes 540672 | tf_op jit(solution)/shard_map/all_gather | solution.py:43
  725.4 0.2 reduce_sum.39
  725.6 0.7 add_divide_fusion
  726.2 6.2 copy.47
  732.4 4.2 slice.12
  736.6 6.2 copy.49
  742.8 8.6 %multiply_add_fusion.1 = f32[54,128,256]{2,1,0:T(8,128)} fusion(f32[54,128,256]{2,1,0:T(8,128)} %param.10, bf16[56,128,256]{2,1,0:T(8,128)(2,1)} %bitcast.53), kind=kLoop, calls=%fused_computation.5 | loop fusion | flops 7077888 | bytes 17694720 | tf_op jit(solution)/shard_map/add | solution.py:71
  751.5 8.6 %multiply_add_fusion = f32[54,128,256]{2,1,0:T(8,128)} fusion(f32[54,128,256]{2,1,0:T(8,128)} %param.11, bf16[56,128,256]{2,1,0:T(8,128)(2,1)} %bitcast.21), kind=kLoop, calls=%fused_computation.4 | loop fusion | flops 7077888 | bytes 17694720 | tf_op jit(solution)/shard_map/add | solution.py:72
  (9 shorter events, 0.0 us)
Async XLA Ops:
  7.2 205.5 %reduce-scatter.2.cloned.1.call-start = ((), (), s32[]{:S(2)}) async-start(), calls=%async_computation.7 | async-start | bytes 35389440 | tf_op jit(solution)/shard_map/reduce_scatter | solution.py:44
  7.2 2.0 copy-start
  11.4 5.8 copy-start.1
  11.4 83.9 %all-to-all-start = ((bf16[8,7,128,256]{3,2,1,0:T(8,128)(2,1)}), bf16[8,7,128,256]{3,2,1,0:T(8,128)(2,1)}, u32[]{:S(2)}, u32[]{:S(2)}) async-start(bf16[8,7,128,256]{3,2,1,0:T(8,128)(2,1)} %bitcast.45), calls=%async_computation.1 | async-start | bytes 7340032 | tf_op jit(solution)/shard_map/all_to_all | solution.py:33
  95.4 85.3 %all-to-all-start.1 = ((bf16[8,7,128,256]{3,2,1,0:T(8,128)(2,1)}), bf16[8,7,128,256]{3,2,1,0:T(8,128)(2,1)}, u32[]{:S(2)}, u32[]{:S(2)}) async-start(bf16[8,7,128,256]{3,2,1,0:T(8,128)(2,1)} %bitcast.44), calls=%async_computation.2 | async-start | bytes 7340032 | tf_op jit(solution)/shard_map/all_to_all | solution.py:33
  103.1 249.8 %all-gather.7.cloned.1.call-start = ((), (), s32[]{:S(2)}) async-start(), calls=%async_computation.9 | async-start | bytes 18350080 | tf_op jit(solution)/shard_map/all_gather | solution.py:62
  212.7 197.7 %all-gather.5.cloned.1.call-start = ((), (), s32[]{:S(2)}) async-start(), calls=%async_computation.8 | async-start | bytes 18350080 | tf_op jit(solution)/shard_map/all_gather | solution.py:52
  439.6 83.1 %all-to-all-start.3 = ((bf16[8,7,128,256]{2,3,1,0:T(8,128)(2,1)}), bf16[8,7,128,256]{2,3,1,0:T(8,128)(2,1)}, u32[]{:S(2)}, u32[]{:S(2)}) async-start(bf16[8,7,128,256]{2,3,1,0:T(8,128)(2,1)} %copy.46), calls=%async_computation.4 | async-start | bytes 7340032 | tf_op jit(solution)/shard_map/all_to_all | solution.py:37
  522.8 85.5 %all-to-all-start.4 = ((bf16[8,7,128,256]{2,3,1,0:T(8,128)(2,1)}), bf16[8,7,128,256]{2,3,1,0:T(8,128)(2,1)}, u32[]{:S(2)}, u32[]{:S(2)}) async-start(bf16[8,7,128,256]{2,3,1,0:T(8,128)(2,1)} %copy.48), calls=%async_computation.5 | async-start | bytes 7340032 | tf_op jit(solution)/shard_map/all_to_all | solution.py:37
  539.9 76.9 %copy-start.2 = (f32[1,1,2,2048]{3,2,1,0:T(2,128)S(1)}, f32[1,1,2,2048]{3,2,1,0:T(2,128)}, u32[]{:S(2)}) copy-start(f32[1,1,2,2048]{3,2,1,0:T(2,128)} %param.14) | copy-start | bytes 49156
  539.9 185.7 %copy-start.3 = (f32[2,2048]{1,0:T(2,128)S(1)}, f32[2,2048]{1,0:T(2,128)}, u32[]{:S(2)}) copy-start(f32[2,2048]{1,0:T(2,128)} %param.15) | copy-start | bytes 49156
  608.2 143.2 %all-to-all-start.5 = ((bf16[8,7,128,256]{3,2,1,0:T(8,128)(2,1)}), bf16[8,7,128,256]{3,2,1,0:T(8,128)(2,1)}, u32[]{:S(2)}, u32[]{:S(2)}) async-start(bf16[8,7,128,256]{3,2,1,0:T(8,128)(2,1)} %bitcast.50), calls=%async_computation.6 | async-start | bytes 7340032 | tf_op jit(solution)/shard_map/all_to_all | solution.py:37
Sparse Core Ops, SparseCore 0:
  10.6 201.9 reduce-scatter.1
  214.8 96.3 all-gather.6
  313.5 96.8 all-gather.4
where the time goes:
time: 768 us; the launch traced here: 767 us
  waiting for transfers between devices  368 us (48%)
  blocking collectives  239 us (31%)
  local copies, waits for them, and re-layouts  40.5 us (5%)
  starting transfers between devices  35.8 us (5%)
  matrix products  35 us (5%)
  other arithmetic  34 us (4%)
  between operations  13.8 us (2%)
    all_to_all x2, waiting for transfers between devices, to_owners(): lax.all_to_all(padded.reshape(n_dp, cap, rows, quarter), 'dp', 0, 0, tile...  149 us
    all_to_all x3, waiting for transfers between devices, to_keepers(): back = lax.all_to_all(owned, 'dp', 0, 0, tiled=True)  133 us
    all_gather x1, blocking collectives, on_device(): norm_grad = jnp.sum(lax.all_gather(local_norm, ('dp', 'group')), axis=0)  109 us
    all_to_all x1, blocking collectives, to_owners(): lax.all_to_all(padded.reshape(n_dp, cap, rows, quarter), 'dp', 0, 0, tile...  85.1 us
    all_gather x1, waiting for transfers between devices, on_device(): piece = lax.all_gather(mine, 'group', axis=2, tiled=True)  57.4 us
    unnamed x1, blocking collectives  40.1 us
    reduce_scatter x1, waiting for transfers between devices, on_device(): lax.psum_scatter(partials[0], 'group', scatter_dimension=2, tiled=True)  27.7 us
    all_to_all x3, starting transfers between devices, to_keepers(): back = lax.all_to_all(owned, 'dp', 0, 0, tiled=True)  22.1 us
  transfers between devices with their start and end apart: 8, of which 6 were waited for; matrix products, arithmetic and copies ran while one was open for 10% of the time, Pallas kernels for 0%

commit v1 on v0

--- a/solution.py
+++ b/solution.py
@@ -49,7 +49,14 @@
     adam_sq = jnp.sum(lax.all_gather(adam_part, ("dp", "group")), axis=0)
     grad_low = grad.astype(jnp.bfloat16)
     mine = to_owners(grad_low)
-    piece = lax.all_gather(mine, "group", axis=2, tiled=True)
+    ring = [mine]
+    for hop in range(3):
+        ring.append(lax.ppermute(ring[-1], "group", [(dev, (dev + 1) % 4) for dev in range(4)]))
+    piece = jnp.roll(
+        jnp.concatenate(ring[::-1], axis=2),
+        (lax.axis_index("group") + 1) * ring[0].shape[2],
+        axis=2,
+    )
     own_rows = lax.dynamic_slice_in_dim(piece, lower, quarter, 1)
     piece4 = piece.reshape(cap, n_dp, rows, width)
     gram_left = jnp.einsum("cdim,cjm->dcij", piece4, own_rows, preferred_element_type=jnp.float32)

time: 768 us -> 939 us (1.22)
  waiting for transfers between devices: 368 us -> 438 us
  blocking collectives: 239 us -> 300 us
  local copies, waits for them, and re-layouts: 40.5 us -> 77 us
    ppermute x0 -> x3, waiting for transfers between devices: none -> 196 us  [on_device(): lax.ppermute(ring[-1], 'group', [(dev, (dev + 1) % 4) for dev in range(4)])]
    all_to_all x3, waiting for transfers between devices: 133 us -> 65.2 us  [to_keepers(): back = lax.all_to_all(owned, 'dp', 0, 0, tiled=True)]
    unnamed x1, blocking collectives: 40.1 us -> 99.6 us
    all_gather x1 -> x0, waiting for transfers between devices: 57.4 us -> none  [on_device(): piece = lax.all_gather(mine, 'group', axis=2, tiled=True)]
    unnamed x10 -> x25, local copies, waits for them, and re-layouts: 1.61 us -> 29.1 us
  transfers between devices with their start and end apart: 8 -> 10, of which waited for: 6 -> 7; matrix products, arithmetic and copies ran while one was open for 10% -> 11% of each run, Pallas kernels for 0% -> 0%
where the time goes in v1:
time: 939 us; the launch traced here: 938 us
  waiting for transfers between devices  438 us (47%)
  blocking collectives  300 us (32%)
  local copies, waits for them, and re-layouts  77 us (8%)
  starting transfers between devices  41.5 us (4%)
  matrix products  36.2 us (4%)
  other arithmetic  29.8 us (3%)
  between operations  14.2 us (2%)
    ppermute x3, waiting for transfers between devices, on_device(): lax.ppermute(ring[-1], 'group', [(dev, (dev + 1) % 4) for dev in range(4)])  196 us
    all_to_all x2, waiting for transfers between devices, to_owners(): lax.all_to_all(padded.reshape(n_dp, cap, rows, quarter), 'dp', 0, 0, tile...  149 us
    all_gather x1, blocking collectives, on_device(): norm_grad = jnp.sum(lax.all_gather(local_norm, ('dp', 'group')), axis=0)  109 us
    unnamed x1, blocking collectives  99.6 us
    all_to_all x1, blocking collectives, to_owners(): lax.all_to_all(padded.reshape(n_dp, cap, rows, quarter), 'dp', 0, 0, tile...  85.1 us
    all_to_all x3, waiting for transfers between devices, to_keepers(): back = lax.all_to_all(owned, 'dp', 0, 0, tiled=True)  65.2 us
    unnamed x25, local copies, waits for them, and re-layouts  29.1 us
    reduce_scatter x1, waiting for transfers between devices, on_device(): lax.psum_scatter(partials[0], 'group', scatter_dimension=2, tiled=True)  27.8 us
  transfers between devices with their start and end apart: 10, of which 7 were waited for; matrix products, arithmetic and copies ran while one was open for 11% of the time, Pallas kernels for 0%

profile of v1, /device:TPU:17, one launch (start us, length us, event | category | flops | bytes accessed | tf_op | source)
XLA Modules:
  0.0 937.6 jit_solution(4889411410901380477)
XLA Ops:
  7.9 1.3 copy-done.2
  9.2 2.2 pad.14
  11.4 5.8 all-to-all-start
  17.3 2.2 pad.15
  19.5 75.9 %all-to-all-done = bf16[8,7,128,256]{3,2,1,0:T(8,128)(2,1)} async-done(((bf16[8,7,128,256]{3,2,1,0:T(8,128)(2,1)}), bf16[8,7,128,256]{3,2,1,0:T(8,128)(2,1)}, u32[]{:S(2)}, u32[]{:S(2)}) %all-to-all-start) | async-done | bytes 3670048 | tf_op jit(solution)/shard_map/all_to_all | solution.py:33
  95.4 7.8 all-to-all-start.1
  103.1 4.3 copy.42
  107.4 73.2 %all-to-all-done.1 = bf16[8,7,128,256]{3,2,1,0:T(8,128)(2,1)} async-done(((bf16[8,7,128,256]{3,2,1,0:T(8,128)(2,1)}), bf16[8,7,128,256]{3,2,1,0:T(8,128)(2,1)}, u32[]{:S(2)}, u32[]{:S(2)}) %all-to-all-start.1) | async-done | bytes 3670048 | tf_op jit(solution)/shard_map/all_to_all | solution.py:33
  180.6 4.2 copy.43
  184.9 27.8 %reduce-scatter.2.cloned.1.call-done = f32[54,128,256]{2,1,0:T(8,128)} async-done(((f32[54,128,1024]{2,1,0:T(8,128)}), f32[54,128,256]{2,1,0:T(8,128)}) %reduce-scatter.2.cloned.1.call-update) | async-done | bytes 7077904 | tf_op jit(solution)/shard_map/reduce_scatter | solution.py:44
  212.6 11.6 %multiply_reduce_fusion.1 = (f32[54]{0:T(128)S(1)}, f32[54,128,256]{2,1,0:T(8,128)}, bf16[54,128,256]{2,1,0:T(8,128)(2,1)S(1)}) fusion(f32[54,128,256]{2,1,0:T(8,128)} %reduce-scatter.2.cloned.1.call-done, f32[54,128,256]{2,1,0:T(8,128)} %param.9), kind=kLoop, calls=%fused_computation.6 | loop fusion | flops 15925194 | bytes 24772824 | tf_op jit(solution)/shard_map/reduce_sum | solution.py:48
  224.8 85.1 %all_to_all.30 = bf16[8,7,128,256]{3,2,1,0:T(8,128)(2,1)S(1)} all-to-all(bf16[8,7,128,256]{3,2,1,0:T(8,128)(2,1)S(1)} %bitcast.46), channel_id=1, replica_groups=mesh['dp'=8,'group'=4] {'dp'}, dimensions={0} | all-to-all | bytes 7340032 | tf_op jit(solution)/shard_map/all_to_all | solution.py:33
  309.9 2.3 copy.44
  312.2 1.7 collective-permute-start
  313.9 96.8 %collective-permute-done = bf16[7,1024,256]{2,1,0:T(8,128)(2,1)} collective-permute-done((bf16[7,1024,256]{2,1,0:T(8,128)(2,1)}, bf16[7,1024,256]{2,1,0:T(8,128)(2,1)}, u32[]{:S(2)}, u32[]{:S(2)}) %collective-permute-start) | collective-permute-done | bytes 3670048 | tf_op jit(solution)/shard_map/ppermute | solution.py:54
  410.7 2.5 collective-permute-start.1
  413.2 58.8 %collective-permute-done.1 = bf16[7,1024,256]{2,1,0:T(8,128)(2,1)} collective-permute-done((bf16[7,1024,256]{2,1,0:T(8,128)(2,1)}, bf16[7,1024,256]{2,1,0:T(8,128)(2,1)}, u32[]{:S(2)}, u32[]{:S(2)}) %collective-permute-start.1) | collective-permute-done | bytes 3670048 | tf_op jit(solution)/shard_map/ppermute | solution.py:54
  472.0 2.5 collective-permute-start.2
  474.4 40.1 %collective-permute-done.2 = bf16[7,1024,256]{2,1,0:T(8,128)(2,1)} collective-permute-done((bf16[7,1024,256]{2,1,0:T(8,128)(2,1)}, bf16[7,1024,256]{2,1,0:T(8,128)(2,1)}, u32[]{:S(2)}, u32[]{:S(2)}) %collective-permute-start.2) | collective-permute-done | bytes 3670048 | tf_op jit(solution)/shard_map/ppermute | solution.py:54
  514.6 2.5 constant_dynamic-update-slice_fusion.7
  517.1 2.6 constant_dynamic-update-slice_fusion.6
  519.7 2.6 constant_dynamic-update-slice_fusion.5
  522.3 2.6 constant_dynamic-update-slice_fusion.4
  524.8 2.6 constant_dynamic-update-slice_fusion.3
  527.4 2.6 constant_dynamic-update-slice_fusion.2
  530.0 2.6 constant_dynamic-update-slice_fusion.1
  532.5 2.6 constant_dynamic-update-slice_fusion
  535.1 9.7 %copy-done.1 = bf16[7,1024,2048]{2,1,0:T(8,128)(2,1)} copy-done((bf16[7,1024,2048]{2,1,0:T(8,128)(2,1)}, bf16[7,1024,2048]{2,1,0:T(8,128)(2,1)S(1)}, u32[]{:S(2)}) %copy-start.1) | copy-done | bytes 29360152
  544.8 6.2 constant_dynamic-slice_fusion
  551.0 8.9 convolution_convert_fusion
  559.9 2.1 copy.58
  562.0 6.0 all-to-all-start.5
  568.0 9.6 %convert_bitcast_fusion = bf16[8,7,128,256]{2,3,0,1:T(8,128)(2,1)S(1)} fusion(bf16[7,8,128,1024]{3,2,1,0:T(8,128)(2,1)} %bitcast.50, bf16[7,1024,2048]{2,1,0:T(8,128)(2,1)} %copy-done.1, s32[]{:T(128)S(6)} %select_n.27, s32[]{:T(128)S(6)} %select_n.28), kind=kOutput, calls=%fused_computation.13 | convolution fusion | flops 3759931392 | bytes 22020104 | tf_op jit(solution)/shard_map/cdim,cjm->dcij/dot_general | solution.py:62
  577.6 2.1 copy.48
  579.7 65.2 %all-to-all-done.5 = bf16[8,7,128,256]{3,2,1,0:T(8,128)(2,1)} async-done(((bf16[8,7,128,256]{3,2,1,0:T(8,128)(2,1)}), bf16[8,7,128,256]{3,2,1,0:T(8,128)(2,1)}, u32[]{:S(2)}, u32[]{:S(2)}) %all-to-all-start.5) | async-done | bytes 3670048 | tf_op jit(solution)/shard_map/all_to_all | solution.py:37
  644.9 9.0 all-to-all-start.4
  654.0 99.6 %all-reduce.4 = f32[1728]{0:T(1024)S(1)} all-reduce(f32[1728]{0:T(1024)S(1)} %dynamic-update-slice), channel_id=2, replica_groups=mesh['dp'=8,'group'=4] {'dp','group'}, use_global_device_ids=true, to_apply=%add.4 | all-reduce | flops 1728 | bytes 13824
  753.8 17.6 %multiply_reduce_fusion = (f32[7]{0:T(128)S(1)}, f32[7,256,8,128]{3,1,2,0:T(8,128)}) fusion(bf16[7,8,128,1024]{3,2,1,0:T(8,128)(2,1)} %bitcast.57, bf16[7,1024,1024]{2,1,0:T(8,128)(2,1)} %constant_dynamic-slice_fusion, bf16[7,1024,256]{2,1,0:T(8,128)(2,1)} %bitcast.55), kind=kOutput, calls=%fused_computation.2 | convolution fusion | flops 7521697792 | bytes 40370204 | tf_op jit(solution)/shard_map/cdim,cmj->dcij/dot_general | solution.py:71
  771.4 7.1 psum.7
  778.6 4.1 fusion.1
  782.8 2.3 copy.46
  785.0 6.3 all-to-all-start.3
  791.3 108.6 %all-gather.1 = f32[32,1,2,2048]{3,2,1,0:T(2,128)S(1)} all-gather(f32[1,1,2,2048]{3,2,1,0:T(2,128)S(1)} %copy-done.4), channel_id=3, replica_groups=mesh['dp'=8,'group'=4] {'dp','group'}, dimensions={0}, use_global_device_ids=true | all-gather | bytes 540672 | tf_op jit(solution)/shard_map/all_gather | solution.py:43
  900.8 6.3 copy.49
  907.1 8.8 multiply_add_fusion
  915.9 4.4 multiply_add_fusion.1
  920.3 6.3 copy.47
  926.6 4.2 slice.12
  (30 shorter events, 2.5 us)
Async XLA Ops:
  7.2 205.5 %reduce-scatter.2.cloned.1.call-start = ((), (), s32[]{:S(2)}) async-start(), calls=%async_computation.7 | async-start | bytes 35389440 | tf_op jit(solution)/shard_map/reduce_scatter | solution.py:44
  7.2 2.0 copy-start.2
  11.4 5.8 copy-start.3
  11.4 83.9 %all-to-all-start = ((bf16[8,7,128,256]{3,2,1,0:T(8,128)(2,1)}), bf16[8,7,128,256]{3,2,1,0:T(8,128)(2,1)}, u32[]{:S(2)}, u32[]{:S(2)}) async-start(bf16[8,7,128,256]{3,2,1,0:T(8,128)(2,1)} %bitcast.45), calls=%async_computation.1 | async-start | bytes 7340032 | tf_op jit(solution)/shard_map/all_to_all | solution.py:33
  95.4 85.3 %all-to-all-start.1 = ((bf16[8,7,128,256]{3,2,1,0:T(8,128)(2,1)}), bf16[8,7,128,256]{3,2,1,0:T(8,128)(2,1)}, u32[]{:S(2)}, u32[]{:S(2)}) async-start(bf16[8,7,128,256]{3,2,1,0:T(8,128)(2,1)} %bitcast.44), calls=%async_computation.2 | async-start | bytes 7340032 | tf_op jit(solution)/shard_map/all_to_all | solution.py:33
  103.1 650.7 %all-gather.4.cloned.1.call-start = ((), (), s32[]{:S(2)}) async-start(), calls=%async_computation.8 | async-start | bytes 18350080 | tf_op jit(solution)/shard_map/all_gather | solution.py:69
  312.2 98.5 %collective-permute-start = (bf16[7,1024,256]{2,1,0:T(8,128)(2,1)}, bf16[7,1024,256]{2,1,0:T(8,128)(2,1)}, u32[]{:S(2)}, u32[]{:S(2)}) collective-permute-start(bf16[7,1024,256]{2,1,0:T(8,128)(2,1)} %bitcast.9), channel_id=1, source_target_pairs={{0,1},{1,2},{2,3},{3,0},{4,5},{5,6},{6,7},{7,4},{8,9},{9,10},{10,1... | collective-permute-start | bytes 11010056 | tf_op jit(solution)/shard_map/ppermute | solution.py:54
  410.7 61.3 %collective-permute-start.1 = (bf16[7,1024,256]{2,1,0:T(8,128)(2,1)}, bf16[7,1024,256]{2,1,0:T(8,128)(2,1)}, u32[]{:S(2)}, u32[]{:S(2)}) collective-permute-start(bf16[7,1024,256]{2,1,0:T(8,128)(2,1)} %collective-permute-done), channel_id=1, source_target_pairs={{0,1},{1,2},{2,3},{3,0},{4,5},{5,6},{6,7},{7,4},{8,9},{9,10},{10,1... | collective-permute-start | bytes 11010056 | tf_op jit(solution)/shard_map/ppermute | solution.py:54
  472.0 42.6 %collective-permute-start.2 = (bf16[7,1024,256]{2,1,0:T(8,128)(2,1)}, bf16[7,1024,256]{2,1,0:T(8,128)(2,1)}, u32[]{:S(2)}, u32[]{:S(2)}) collective-permute-start(bf16[7,1024,256]{2,1,0:T(8,128)(2,1)} %collective-permute-done.1), channel_id=1, source_target_pairs={{0,1},{1,2},{2,3},{3,0},{4,5},{5,6},{6,7},{7,4},{8,9},{9,10},{10,1... | collective-permute-start | bytes 11010056 | tf_op jit(solution)/shard_map/ppermute | solution.py:54
  535.1 9.7 %copy-start.1 = (bf16[7,1024,2048]{2,1,0:T(8,128)(2,1)}, bf16[7,1024,2048]{2,1,0:T(8,128)(2,1)S(1)}, u32[]{:S(2)}) copy-start(bf16[7,1024,2048]{2,1,0:T(8,128)(2,1)S(1)} %constant_dynamic-update-slice_fusion) | copy-start | bytes 88080384
  562.0 82.8 %all-to-all-start.5 = ((bf16[8,7,128,256]{3,2,1,0:T(8,128)(2,1)}), bf16[8,7,128,256]{3,2,1,0:T(8,128)(2,1)}, u32[]{:S(2)}, u32[]{:S(2)}) async-start(bf16[8,7,128,256]{3,2,1,0:T(8,128)(2,1)} %bitcast.48), calls=%async_computation.6 | async-start | bytes 7340032 | tf_op jit(solution)/shard_map/all_to_all | solution.py:37
  644.9 140.2 %all-to-all-start.4 = ((bf16[8,7,128,256]{2,3,1,0:T(8,128)(2,1)}), bf16[8,7,128,256]{2,3,1,0:T(8,128)(2,1)}, u32[]{:S(2)}, u32[]{:S(2)}) async-start(bf16[8,7,128,256]{2,3,1,0:T(8,128)(2,1)} %copy.48), calls=%async_computation.5 | async-start | bytes 7340032 | tf_op jit(solution)/shard_map/all_to_all | solution.py:37
  782.7 8.6 copy-start.4
  782.7 117.4 %copy-start.5 = (f32[2,2048]{1,0:T(2,128)S(1)}, f32[2,2048]{1,0:T(2,128)}, u32[]{:S(2)}) copy-start(f32[2,2048]{1,0:T(2,128)} %param.15) | copy-start | bytes 49156
  785.0 135.2 %all-to-all-start.3 = ((bf16[8,7,128,256]{2,3,1,0:T(8,128)(2,1)}), bf16[8,7,128,256]{2,3,1,0:T(8,128)(2,1)}, u32[]{:S(2)}, u32[]{:S(2)}) async-start(bf16[8,7,128,256]{2,3,1,0:T(8,128)(2,1)} %copy.46), calls=%async_computation.4 | async-start | bytes 7340032 | tf_op jit(solution)/shard_map/all_to_all | solution.py:37
  900.8 15.1 %slice-start = ((s8[7077888]{0:T(1024)(128)(4,1)}), s8[2883584]{0:T(1024)(128)(4,1)S(1)}, s32[]{:S(2)}) async-start(s8[7077888]{0:T(1024)(128)(4,1)} %bitcast.53), calls=%async_computation.9 | async-start | bytes 5767168
  907.1 8.8 copy-start
  907.1 8.8 slice-start.1
Sparse Core Ops, SparseCore 0:
  10.6 201.9 reduce-scatter.1
  314.0 133.9 all-gather.3
